TPU v7x, 256 devices: a whole 4x4x8 slice. The times are simulated.
256 devices in a mesh: rep: 16 (over x, y_lo, core), blk: 16 (over y_hi, z).
Axes of the slice: x: 4, y: 4 (y_hi: 2, y_lo: 2; y = y_hi * 2 + y_lo), z: 8, core: 2. Of those that a mesh axis runs over, the one named last changes fastest.
Arguments:
- features: bfloat16 [65536, 1024], P(('rep', 'blk')), may hold values from -6 to 6
- weight: bfloat16 [1024, 1024], replicated, may hold values from -0.1875 to 0.1875
- bias: bfloat16 [1024], replicated, may hold values from -3 to 3
- tile_vals: bfloat16 [16, 16, 32, 4, 128, 128], P('rep', 'blk'), may hold values from -0.125 to 0.125
- tile_col: int32 [16, 16, 32, 4], P('rep', 'blk'), may hold values from 0 to 31
- tile_count: int32 [16, 16, 32], P('rep', 'blk'), may hold values from 0 to 4, as said below
Outputs:
- hidden: bfloat16 [65536, 1024], P(('rep', 'blk'))
Inputs may be any that keep to these rules, and one draw needn't show every extreme that they name: The first tile_count slots are the live ones; some entry equals 4 in every draw.
All inputs are finite; a program needn't handle non-finite values.
Results may differ from a plain program's by a relative error of at most 0.014.
Values may be sent and summed in bfloat16 or wider, within the bound.
No kernel may reach another device: no remote copies, remote signals or barrier semaphores. Data moves between devices by JAX's collectives and lax.ppermute only.
A program may use at most 64 MiB of HBM per device.

v0:
```python
import jax
import jax.numpy as jnp
from jax import lax
from jax.sharding import PartitionSpec as P


def term_maker(gathered, tile_block, col_index, live_count):
    tile_side = tile_block.shape[-1]
    slot_total = tile_block.shape[1]
    sources = gathered.reshape(-1, tile_side, gathered.shape[1])

    def block_sum(blk_id):
        block_tiles = tile_block[blk_id]
        block_cols = col_index[blk_id]
        block_live = live_count[blk_id]
        keep_mask = (jnp.arange(slot_total, dtype=jnp.int32) < block_live).astype(jnp.bfloat16)
        masked = block_tiles * keep_mask[:, None, None]
        picked = sources[block_cols]
        return jnp.einsum("kij,kjd->id", masked, picked, preferred_element_type=jnp.float32)

    def partial_term(start, count):
        block_ids = jnp.arange(count // tile_side, dtype=jnp.int32)
        return lax.map(block_sum, block_ids).reshape(count, -1)

    return partial_term


def body(features, weight, bias, tile_vals, tile_col, tile_count):
    tile_block = tile_vals[0, 0]
    col_index = tile_col[0, 0]
    live_count = tile_count[0, 0]
    row_total = features.shape[0]
    gathered = lax.all_gather(features, "rep", axis=0, tiled=True)
    summer = term_maker(gathered, tile_block, col_index, live_count)
    summed = lax.psum_scatter(
        summer(jnp.int32(0), row_total * lax.axis_size("blk")).astype(jnp.bfloat16),
        "blk",
        scatter_dimension=0,
        tiled=True,
    )
    mixed = jnp.dot(summed, weight, preferred_element_type=jnp.float32) + bias.astype(jnp.float32)
    return jnp.maximum(mixed, 0.0).astype(jnp.bfloat16)


def solution(mesh):
    return jax.shard_map(
        body,
        mesh=mesh,
        in_specs=(
            P(("rep", "blk"), None),
            P(),
            P(),
            P("rep", "blk", None, None, None, None),
            P("rep", "blk", None, None),
            P("rep", "blk", None),
        ),
        out_specs=P(("rep", "blk"), None),
        check_vma=False,
    )
```

profile of v0, /device:TPU:2, one launch (start us, length us, event | category | flops | bytes accessed | tf_op | source)
XLA Modules:
  0.0 625.8 jit_solution(16292536515272177173)
XLA Ops:
  8.1 58.6 %all-gather.2.cloned.1.call-done = bf16[4096,1024]{1,0:T(8,128)(2,1)} async-done(((bf16[256,1024]{1,0:T(8,128)(2,1)}), bf16[4096,1024]{1,0:T(8,128)(2,1)}) %all-gather.2.cloned.1.call-update) | async-done | bytes 8388624 | tf_op jit(solution)/shard_map/all_gather | solution.py:33
  66.7 322.8 %while.10 = (s32[]{:T(128)}, bf16[32,128,1024]{2,1,0:T(8,128)(2,1)}, s32[32]{0:T(128)S(1)}, bf16[32,4,128,128]{3,2,1,0:T(8,128)(2,1)}, s32[32]{0:T(128)}, /*inde...) while((s32[]{:T(128)}, bf16[32,128,1024]{2,1,0:T(8,128)(2,1)}, ...), condition=%wide.region_1.2_spmd, body=%wide.region_0.1_spmd.sunk | while | flops 134284320 | bytes 3805947 | solution.py:23
  69.0 4.0 gather_fusion
  79.1 4.0 gather_fusion
  89.2 4.0 gather_fusion
  99.3 4.0 gather_fusion
  109.4 4.0 gather_fusion
  119.4 4.0 gather_fusion
  129.5 4.0 gather_fusion
  139.6 4.0 gather_fusion
  149.7 4.0 gather_fusion
  159.8 4.0 gather_fusion
  169.9 4.0 gather_fusion
  179.9 4.0 gather_fusion
  190.0 4.0 gather_fusion
  200.1 4.0 gather_fusion
  210.2 4.0 gather_fusion
  220.3 4.0 gather_fusion
  230.3 4.0 gather_fusion
  240.4 4.0 gather_fusion
  250.5 4.0 gather_fusion
  260.7 4.0 gather_fusion
  270.7 4.0 gather_fusion
  280.8 4.0 gather_fusion
  290.9 4.0 gather_fusion
  301.0 4.0 gather_fusion
  311.0 4.0 gather_fusion
  321.1 4.0 gather_fusion
  331.2 4.0 gather_fusion
  341.3 4.0 gather_fusion
  361.5 4.0 gather_fusion
  390.1 226.2 %reduce-scatter.2.cloned.1.call-done = bf16[256,1024]{1,0:T(8,128)(2,1)} async-done(((bf16[4096,1024]{1,0:T(8,128)(2,1)}), bf16[256,1024]{1,0:T(8,128)(2,1)}) %reduce-scatter.2.cloned.1.call-update) | async-done | bytes 524304 | tf_op jit(solution)/shard_map/reduce_scatter | solution.py:35
  (208 shorter events, 156.6 us)
Async XLA Ops:
  6.5 609.8 %copy-start = (bf16[1024,1024]{1,0:T(8,128)(2,1)S(1)}, bf16[1024,1024]{1,0:T(8,128)(2,1)}, u32[]{:S(2)}) copy-start(bf16[1024,1024]{1,0:T(8,128)(2,1)} %param.9) | copy-start | bytes 6291460
  6.5 60.1 %all-gather.2.cloned.1.call-start = ((), (), s32[]{:S(2)}) async-start(), calls=%async_computation.1 | async-start | bytes 8912896 | tf_op jit(solution)/shard_map/all_gather | solution.py:33
  7.3 609.1 %reduce-scatter.2.cloned.1.call-start = ((), (), s32[]{:S(2)}) async-start(), calls=%async_computation.2 | async-start | bytes 8912896 | tf_op jit(solution)/shard_map/reduce_scatter | solution.py:35
  389.4 0.7 copy-start.1
Sparse Core Ops, SparseCore 0:
  9.2 57.4 all-gather.1
  389.6 226.7 reduce-scatter.1
where the time goes:
time: 629 us; the launch traced here: 626 us
  waiting for transfers between devices  286 us (45%)
  local copies, waits for them, and re-layouts  187 us (30%)
  matrix products  65.6 us (10%)
  loops' own time  55.1 us (9%)
  other arithmetic  18.6 us (3%)
  between operations  13.4 us (2%)
    reduce_scatter x1, waiting for transfers between devices, body(): lax.psum_scatter(summer(jnp.int32(0), row_total * lax.axis_size('blk')).a...  226 us
    gather x32, local copies, waits for them, and re-layouts, block_sum(): picked = sources[block_cols]  128 us
    dot_general x32, matrix products, block_sum(): jnp.einsum('kij,kjd->id', masked, picked, preferred_element_type=jnp.floa...  63.1 us
    all_gather x1, waiting for transfers between devices, body(): gathered = lax.all_gather(features, 'rep', axis=0, tiled=True)  58.6 us
    another operation x1, loops' own time, partial_term(): return lax.map(block_sum, block_ids).reshape(count, -1)  55.1 us
    dynamic_slice x32, local copies, waits for them, and re-layouts, block_sum(): block_live = live_count[blk_id]  39.6 us
    dynamic_slice x32, local copies, waits for them, and re-layouts, partial_term(): return lax.map(block_sum, block_ids).reshape(count, -1)  18.5 us
    convert_element_type x32, other arithmetic, block_sum(): (jnp.arange(slot_total, dtype=jnp.int32) < block_live).astype(jnp.bfloat16)  18 us
  transfers between devices with their start and end apart: 2, of which 2 were waited for; matrix products, arithmetic and copies ran while one was open for 0% of the time, Pallas kernels for 0%

commit v1 on v0

--- a/solution.py
+++ b/solution.py
@@ -30,7 +30,9 @@
     col_index = tile_col[0, 0]
     live_count = tile_count[0, 0]
     row_total = features.shape[0]
-    gathered = lax.all_gather(features, "rep", axis=0, tiled=True)
+    gathered = jnp.concatenate(
+        lax.all_to_all(jnp.stack([features] * lax.axis_size("rep")), "rep", 0, 0), axis=0
+    )
     summer = term_maker(gathered, tile_block, col_index, live_count)
     summed = lax.psum_scatter(
         summer(jnp.int32(0), row_total * lax.axis_size("blk")).astype(jnp.bfloat16),

time: 629 us -> 715 us (1.14)
  waiting for transfers between devices: 286 us -> 359 us
  loops' own time: 55.1 us -> 67.2 us
  local copies, waits for them, and re-layouts: 187 us -> 177 us
    all_to_all x0 -> x1, waiting for transfers between devices: none -> 99.4 us  [body(): lax.all_to_all(jnp.stack([features] * lax.axis_size('rep')), 'rep', 0, 0)]
    all_gather x1 -> x0, waiting for transfers between devices: 58.6 us -> none  [body(): gathered = lax.all_gather(features, 'rep', axis=0, tiled=True)]
    reduce_scatter x1, waiting for transfers between devices: 226 us -> 260 us  [body(): lax.psum_scatter(summer(jnp.int32(0), row_total * lax.axis_size('blk')).a...]
    dynamic_slice x32, local copies, waits for them, and re-layouts: 39.6 us -> 21.3 us  [block_sum(): block_live = live_count[blk_id]]
    another operation x1, loops' own time: 55.1 us -> 67.2 us  [partial_term(): return lax.map(block_sum, block_ids).reshape(count, -1)]
where the time goes in v1:
time: 715 us; the launch traced here: 711 us
  waiting for transfers between devices  359 us (50%)
  local copies, waits for them, and re-layouts  177 us (25%)
  loops' own time  67.2 us (9%)
  matrix products  65.5 us (9%)
  other arithmetic  22.6 us (3%)
  between operations  13.4 us (2%)
    reduce_scatter x1, waiting for transfers between devices, body(): lax.psum_scatter(summer(jnp.int32(0), row_total * lax.axis_size('blk')).a...  260 us
    gather x32, local copies, waits for them, and re-layouts, block_sum(): picked = sources[block_cols]  128 us
    all_to_all x1, waiting for transfers between devices, body(): lax.all_to_all(jnp.stack([features] * lax.axis_size('rep')), 'rep', 0, 0)  99.4 us
    another operation x1, loops' own time, partial_term(): return lax.map(block_sum, block_ids).reshape(count, -1)  67.2 us
    dot_general x32, matrix products, block_sum(): jnp.einsum('kij,kjd->id', masked, picked, preferred_element_type=jnp.floa...  63 us
    convert_element_type x32, other arithmetic, block_sum(): (jnp.arange(slot_total, dtype=jnp.int32) < block_live).astype(jnp.bfloat16)  22.1 us
    dynamic_slice x32, local copies, waits for them, and re-layouts, block_sum(): block_live = live_count[blk_id]  21.3 us
    dynamic_slice x32, local copies, waits for them, and re-layouts, partial_term(): return lax.map(block_sum, block_ids).reshape(count, -1)  21.1 us
  transfers between devices with their start and end apart: 2, of which 2 were waited for; matrix products, arithmetic and copies ran while one was open for 0% of the time, Pallas kernels for 0%

profile of v1, /device:TPU:2, one launch (start us, length us, event | category | flops | bytes accessed | tf_op | source)
XLA Modules:
  0.0 711.2 jit_solution(17492783388286250130)
XLA Ops:
  6.5 5.5 stack.2
  12.0 6.9 all-to-all-start
  19.1 99.4 %all-to-all-done = bf16[16,256,1024]{2,1,0:T(8,128)(2,1)} async-done(((bf16[16,256,1024]{2,1,0:T(8,128)(2,1)}), bf16[16,256,1024]{2,1,0:T(8,128)(2,1)}, u32[]{:S(2)}, u32[]{:S(2)}) %all-to-all-start) | async-done | bytes 8388640 | tf_op jit(solution)/shard_map/all_to_all | solution.py:34
  118.5 323.1 %while.10 = (s32[]{:T(128)}, bf16[32,128,1024]{2,1,0:T(8,128)(2,1)}, s32[32]{0:T(128)S(1)}, bf16[32,4,128,128]{3,2,1,0:T(8,128)(2,1)}, s32[32]{0:T(128)S(1)}, /*...) while((s32[]{:T(128)}, bf16[32,128,1024]{2,1,0:T(8,128)(2,1)}, ...), condition=%wide.region_1.2_spmd, body=%wide.region_0.1_spmd.sunk | while | flops 134284320 | bytes 3805947 | solution.py:23
  121.2 4.0 gather_fusion
  131.4 4.0 gather_fusion
  141.5 4.0 gather_fusion
  151.6 4.0 gather_fusion
  161.7 4.0 gather_fusion
  171.8 4.0 gather_fusion
  181.9 4.0 gather_fusion
  191.9 4.0 gather_fusion
  202.0 4.0 gather_fusion
  212.1 4.0 gather_fusion
  222.2 4.0 gather_fusion
  232.3 4.0 gather_fusion
  242.4 4.0 gather_fusion
  252.5 4.0 gather_fusion
  262.6 4.0 gather_fusion
  272.7 4.0 gather_fusion
  282.8 4.0 gather_fusion
  292.9 4.0 gather_fusion
  303.0 4.0 gather_fusion
  313.1 4.0 gather_fusion
  323.2 4.0 gather_fusion
  333.3 4.0 gather_fusion
  343.4 4.0 gather_fusion
  353.5 4.0 gather_fusion
  363.5 4.0 gather_fusion
  373.7 4.0 gather_fusion
  383.7 4.0 gather_fusion
  442.2 259.6 %reduce-scatter.2.cloned.1.call-done = bf16[256,1024]{1,0:T(8,128)(2,1)} async-done(((bf16[4096,1024]{1,0:T(8,128)(2,1)}), bf16[256,1024]{1,0:T(8,128)(2,1)}) %reduce-scatter.2.cloned.1.call-update) | async-done | bytes 524304 | tf_op jit(solution)/shard_map/reduce_scatter | solution.py:37
  (212 shorter events, 151.3 us)
Async XLA Ops:
  6.5 695.3 %copy-start = (bf16[1024,1024]{1,0:T(8,128)(2,1)S(1)}, bf16[1024,1024]{1,0:T(8,128)(2,1)}, u32[]{:S(2)}) copy-start(bf16[1024,1024]{1,0:T(8,128)(2,1)} %param.9) | copy-start | bytes 6291460
  12.0 6.9 copy-start.1
  12.0 106.4 %copy-start.3 = (s32[1,1,32]{2,1,0:T(1,128)S(1)}, s32[1,1,32]{2,1,0:T(1,128)}, u32[]{:S(2)}) copy-start(s32[1,1,32]{2,1,0:T(1,128)} %param.13) | copy-start | bytes 388
  12.0 106.4 %all-to-all-start = ((bf16[16,256,1024]{2,1,0:T(8,128)(2,1)}), bf16[16,256,1024]{2,1,0:T(8,128)(2,1)}, u32[]{:S(2)}, u32[]{:S(2)}) async-start(bf16[16,256,1024]{2,1,0:T(8,128)(2,1)} %stack.2), calls=%async_computation | async-start | bytes 16777216 | tf_op jit(solution)/shard_map/all_to_all | solution.py:34
  18.9 682.9 %reduce-scatter.2.cloned.1.call-start = ((), (), s32[]{:S(2)}) async-start(), calls=%async_computation.2 | async-start | bytes 8912896 | tf_op jit(solution)/shard_map/reduce_scatter | solution.py:37
  441.5 0.7 copy-start.2
Sparse Core Ops, SparseCore 0:
  441.7 260.1 reduce-scatter.1
